TPU v7x, 32 devices: a whole 2x2x4 slice. The times are simulated.
32 devices in a mesh: mem: 8 (over z, y), head: 4 (over x, core).
Axes of the slice: x: 2, y: 2, z: 4, core: 2. Of those that a mesh axis runs over, the one named last changes fastest.
Arguments:
- queries: bfloat16 [4096, 2048], P('mem', 'head'), may hold values from -8 to 8
- local_keys: bfloat16 [4096, 2048], P('mem', 'head'), may hold values from -8 to 8
- local_values: bfloat16 [4096, 2048], P('mem', 'head'), may hold values from -8 to 8
- memory_keys: bfloat16 [128, 32, 2048], P('mem', None, 'head'), may hold values from -8 to 8
- memory_values: bfloat16 [128, 32, 2048], P('mem', None, 'head'), may hold values from -8 to 8
- retrieval: int32 [8, 32], replicated, may hold values from 0 to 127, as said below
- gate_logit: float32 [16], P('head'), may hold values from -4 to 4
- dropout_keep: int32 [4096, 2048], P('mem', 'head'), may hold values 0 or 1
- out_weight: bfloat16 [2048, 2048], P('head'), may hold values from -0.125 to 0.125
- cotangent: bfloat16 [4096, 2048], P('mem', 'head'), may hold values from -6 to 6
Outputs:
- layer_out: bfloat16 [4096, 2048], P('mem', 'head')
- grad_queries: bfloat16 [4096, 2048], P('mem', 'head')
- grad_keys: bfloat16 [4096, 2048], P('mem', 'head')
- grad_values: bfloat16 [4096, 2048], P('mem', 'head')
- grad_memory_keys: bfloat16 [128, 32, 2048], P('mem', None, 'head')
- grad_memory_values: bfloat16 [128, 32, 2048], P('mem', None, 'head')
Inputs may be any that keep to these rules, and one draw needn't show every extreme that they name: `retrieval`: block i lies on shard i // 16. Rows d * 1 to (d + 1) - 1 belong to index d of mem; together they name 32 distinct blocks, at most 8 of them on any one shard, and in every draw one shard receives exactly 8 from the rows of every index.
All inputs are finite; a program needn't handle non-finite values. No bound on the sum of `dropout_keep` on one device may be relied on, other than what follows from the above.
Results may differ from a plain program's by a relative error of at most 0.0079.
Values may be sent and summed in bfloat16 or wider, within the bound.
No kernel may reach another device: no remote copies, remote signals or barrier semaphores. Data moves between devices by JAX's collectives and lax.ppermute only.
A program may use at most 128 MiB of HBM per device.

v0:
```python
import jax
import jax.numpy as jnp
from jax import lax
from jax.sharding import PartitionSpec as P

QBLK = 512
keep_scale = 1.0 / 0.9


def contract_last(left, right):
    return lax.dot_general(
        left, right, (((1,), (1,)), ((), ())), preferred_element_type=jnp.float32
    )


def contract_first(left, right):
    return lax.dot_general(
        left, right, (((0,), (0,)), ((), ())), preferred_element_type=jnp.float32
    )


def branch_weights(query_rows, keyset, causal):
    score_scale = query_rows.shape[1] ** (-0.5)
    scores = contract_last(query_rows, keyset) * score_scale
    if causal:
        row_iota = lax.broadcasted_iota(jnp.int32, scores.shape, 0)
        col_iota = lax.broadcasted_iota(jnp.int32, scores.shape, 1)
        scores = jnp.where(col_iota <= row_iota, scores, -jnp.inf)
    return jnp.exp(scores - jnp.max(scores, axis=1, keepdims=True))


def branch_forward(query_rows, keyset, valueset, causal):
    weights = branch_weights(query_rows, keyset, causal)
    row_total = jnp.sum(weights, axis=1, keepdims=True)
    mixed_out = (
        jnp.dot(weights.astype(jnp.bfloat16), valueset, preferred_element_type=jnp.float32)
        / row_total
    )
    return (mixed_out, row_total)


def branch_backward(query_rows, keyset, valueset, row_total, mixed_out, grad_mixed, causal):
    weights = branch_weights(query_rows, keyset, causal)
    probabilities = weights / row_total
    delta_rows = jnp.sum(grad_mixed * mixed_out, axis=1, keepdims=True)
    grad_low = grad_mixed.astype(jnp.bfloat16)
    grad_probs = contract_last(grad_low, valueset)
    score_scale = query_rows.shape[1] ** (-0.5)
    grad_scores = (probabilities * (grad_probs - delta_rows) * score_scale).astype(jnp.bfloat16)
    grad_query = jnp.dot(grad_scores, keyset, preferred_element_type=jnp.float32)
    grad_keyset = contract_first(grad_scores, query_rows)
    grad_valueset = contract_first(probabilities.astype(jnp.bfloat16), grad_low)
    return (grad_query, grad_keyset, grad_valueset)


def per_device(
    queries,
    local_keys,
    local_values,
    memory_keys,
    memory_values,
    retrieval,
    gate_logit,
    dropout_keep,
    out_weight,
    cotangent,
):
    mem_count = lax.axis_size("mem")
    mem_index = lax.axis_index("mem")
    tok_rows, feature_cols = queries.shape
    heads_here = gate_logit.shape[0]
    head_dim = feature_cols // heads_here
    blocks_here = memory_keys.shape[0]
    block_len = memory_keys.shape[1]
    query_blocks = tok_rows // QBLK
    top_blocks = retrieval.shape[1]
    request_count = query_blocks * top_blocks
    capacity = 2 * request_count // mem_count
    slot_count = mem_count * capacity
    entries = block_len * feature_cols
    owner_ids = retrieval // blocks_here
    local_ids = retrieval % blocks_here
    earlier_mask = lax.broadcasted_iota(
        jnp.int32, (request_count, request_count), 0
    ) < lax.broadcasted_iota(jnp.int32, (request_count, request_count), 1)
    same_owner = owner_ids[:, :, None] == owner_ids[:, None, :]
    owner_rank = jnp.sum((same_owner & earlier_mask[None]).astype(jnp.int32), axis=1)
    request_owner = lax.dynamic_index_in_dim(owner_ids, mem_index, 0, keepdims=False)
    request_rank = lax.dynamic_index_in_dim(owner_rank, mem_index, 0, keepdims=False)
    request_slot = request_owner * capacity + request_rank
    slot_iota = lax.broadcasted_iota(jnp.int32, (request_count, slot_count), 1)
    pick_table = (request_slot[:, None] == slot_iota).astype(jnp.bfloat16)
    cap_iota = lax.broadcasted_iota(jnp.int32, (mem_count, request_count, capacity), 2)
    wanted = (owner_ids[:, :, None] == mem_index) & (owner_rank[:, :, None] == cap_iota)
    send_local = jnp.sum(wanted.astype(jnp.int32) * (local_ids[:, :, None] + 1), axis=1) - 1
    block_iota = lax.broadcasted_iota(jnp.int32, (slot_count, blocks_here), 1)
    serve_table = (send_local.reshape(slot_count, 1) == block_iota).astype(jnp.bfloat16)

    def outgoing(table):
        flat_rows = table.reshape(blocks_here, entries)
        served = jnp.dot(serve_table, flat_rows, preferred_element_type=jnp.float32)
        return served.astype(jnp.bfloat16).reshape(mem_count, capacity, block_len, feature_cols)

    def selected(blocks):
        flat_rows = blocks.reshape(slot_count, entries)
        chosen = jnp.dot(pick_table, flat_rows, preferred_element_type=jnp.float32)
        return chosen.astype(jnp.bfloat16).reshape(top_blocks * block_len, feature_cols)

    fetched = (
        lax.all_to_all(outgoing(memory_keys), "mem", split_axis=0, concat_axis=0, tiled=True),
        lax.all_to_all(outgoing(memory_values), "mem", split_axis=0, concat_axis=0, tiled=True),
    )
    gate_values = 1.0 / (1.0 + jnp.exp(-gate_logit))
    keep_mask = dropout_keep.astype(jnp.float32)
    saved_state = []
    block_index = 0
    row_start = block_index * QBLK
    row_stop = row_start + QBLK
    mem_keyset = selected(fetched[0])
    mem_valueset = selected(fetched[1])
    head_parts = []
    for head_index in range(heads_here):
        col_start = head_index * head_dim
        col_stop = col_start + head_dim
        query_rows = queries[row_start:row_stop, col_start:col_stop]
        mixed_loc, total_loc = branch_forward(
            query_rows,
            local_keys[row_start:row_stop, col_start:col_stop],
            local_values[row_start:row_stop, col_start:col_stop],
            True,
        )
        mixed_mem, total_mem = branch_forward(
            query_rows,
            mem_keyset[:, col_start:col_stop],
            mem_valueset[:, col_start:col_stop],
            False,
        )
        saved_state.append((mixed_loc, total_loc, mixed_mem, total_mem))
        head_parts.append(
            gate_values[head_index] * mixed_mem + (1.0 - gate_values[head_index]) * mixed_loc
        )
    attended_parts = jnp.concatenate(head_parts, axis=1)
    dropped = (attended_parts * keep_mask * keep_scale).astype(jnp.bfloat16)
    partial_out = jnp.dot(dropped, out_weight, preferred_element_type=jnp.float32)
    layer_out = lax.psum_scatter(partial_out, "head", scatter_dimension=1, tiled=True).astype(
        jnp.bfloat16
    )
    cotangent_full = lax.all_gather(cotangent, "head", axis=1, tiled=True)
    grad_attended = contract_last(cotangent_full, out_weight) * keep_mask * keep_scale
    query_grads, key_grads, value_grads, memkey_parts, memvalue_parts = ([], [], [], [], [])
    block_index = 0
    row_start = block_index * QBLK
    row_stop = row_start + QBLK
    mem_keyset = selected(fetched[0])
    mem_valueset = selected(fetched[1])
    head_query = []
    head_key = []
    head_value = []
    head_memkey = []
    head_memvalue = []
    for head_index in range(heads_here):
        col_start = head_index * head_dim
        col_stop = col_start + head_dim
        mixed_loc, total_loc, mixed_mem, total_mem = saved_state[
            block_index * heads_here + head_index
        ]
        query_rows = queries[row_start:row_stop, col_start:col_stop]
        grad_here = grad_attended[row_start:row_stop, col_start:col_stop]
        query_mem, keyset_mem, valueset_mem = branch_backward(
            query_rows,
            mem_keyset[:, col_start:col_stop],
            mem_valueset[:, col_start:col_stop],
            total_mem,
            mixed_mem,
            gate_values[head_index] * grad_here,
            False,
        )
        query_loc, keyset_loc, valueset_loc = branch_backward(
            query_rows,
            local_keys[row_start:row_stop, col_start:col_stop],
            local_values[row_start:row_stop, col_start:col_stop],
            total_loc,
            mixed_loc,
            (1.0 - gate_values[head_index]) * grad_here,
            True,
        )
        head_query.append((query_mem + query_loc).astype(jnp.bfloat16))
        head_key.append(keyset_loc.astype(jnp.bfloat16))
        head_value.append(valueset_loc.astype(jnp.bfloat16))
        head_memkey.append(keyset_mem.astype(jnp.bfloat16))
        head_memvalue.append(valueset_mem.astype(jnp.bfloat16))
    query_grads.append(jnp.concatenate(head_query, axis=1))
    key_grads.append(jnp.concatenate(head_key, axis=1))
    value_grads.append(jnp.concatenate(head_value, axis=1))
    memkey_parts.append(jnp.concatenate(head_memkey, axis=1).reshape(top_blocks, entries))
    memvalue_parts.append(jnp.concatenate(head_memvalue, axis=1).reshape(top_blocks, entries))
    send_keys = contract_first(pick_table, memkey_parts[0]).astype(jnp.bfloat16)
    send_values = contract_first(pick_table, memvalue_parts[0]).astype(jnp.bfloat16)
    returned = (
        lax.all_to_all(
            send_keys.reshape(mem_count, capacity, block_len, feature_cols),
            "mem",
            split_axis=0,
            concat_axis=0,
            tiled=True,
        ),
        lax.all_to_all(
            send_values.reshape(mem_count, capacity, block_len, feature_cols),
            "mem",
            split_axis=0,
            concat_axis=0,
            tiled=True,
        ),
    )
    grad_memory_keys = contract_first(serve_table, returned[0].reshape(slot_count, entries)).astype(
        jnp.bfloat16
    )
    grad_memory_values = contract_first(
        serve_table, returned[1].reshape(slot_count, entries)
    ).astype(jnp.bfloat16)
    return (
        layer_out,
        query_grads[0],
        key_grads[0],
        value_grads[0],
        grad_memory_keys.reshape(blocks_here, block_len, feature_cols),
        grad_memory_values.reshape(blocks_here, block_len, feature_cols),
    )


def solution(mesh):
    placed = (
        P("mem", "head"),
        P("mem", "head"),
        P("mem", "head"),
        P("mem", None, "head"),
        P("mem", None, "head"),
        P(),
        P("head"),
        P("mem", "head"),
        P("head", None),
        P("mem", "head"),
    )
    return jax.shard_map(
        per_device,
        mesh=mesh,
        in_specs=placed,
        out_specs=(
            P("mem", "head"),
            P("mem", "head"),
            P("mem", "head"),
            P("mem", "head"),
            P("mem", None, "head"),
            P("mem", None, "head"),
        ),
        check_vma=False,
    )
```

profile of v0, /device:TPU:0, one launch (start us, length us, event | category | flops | bytes accessed | tf_op | source)
XLA Modules:
  0.0 273.9 jit_solution(1934526136832263948)
XLA Ops:
  10.5 2.1 convolution_convert_fusion.3
  12.6 7.4 %all-to-all-start = ((bf16[8,8,32,512]{3,1,2,0:T(8,128)(2,1)}), bf16[8,8,32,512]{3,1,2,0:T(8,128)(2,1)}, u32[]{:S(2)}, u32[]{:S(2)}) async-start(bf16[8,8,32,512]{3,1,2,0:T(8,128)(2,1)} %bitcast.85), calls=%async_computation | async-start | bytes 4194304 | tf_op jit(solution)/shard_map/all_to_all | solution.py:110
  27.8 2.1 convolution_convert_fusion.2
  29.9 38.5 %all-to-all-done = bf16[8,8,32,512]{3,1,2,0:T(8,128)(2,1)} async-done(((bf16[8,8,32,512]{3,1,2,0:T(8,128)(2,1)}), bf16[8,8,32,512]{3,1,2,0:T(8,128)(2,1)}, u32[]{:S(2)}, u32[]{:S(2)}) %all-to-all-start) | async-done | bytes 2097184 | tf_op jit(solution)/shard_map/all_to_all | solution.py:110
  68.4 4.3 %all-to-all-start.1 = ((bf16[8,8,32,512]{3,1,2,0:T(8,128)(2,1)}), bf16[8,8,32,512]{3,1,2,0:T(8,128)(2,1)}, u32[]{:S(2)}, u32[]{:S(2)}) async-start(bf16[8,8,32,512]{3,1,2,0:T(8,128)(2,1)} %bitcast.84), calls=%async_computation.1 | async-start | bytes 4194304 | tf_op jit(solution)/shard_map/all_to_all | solution.py:111
  75.2 2.5 copy.42
  85.4 3.0 %fusion.8 = f32[512,512]{0,1:T(8,128)S(1)} fusion(bf16[512,2048]{1,0:T(8,128)(2,1)} %all-gather.2.cloned.1.call-done, bf16[512,2048]{1,0:T(8,128)(2,1)S(1)} %copy-done, s32[512,512]{0,1:T(8,128)S(1)} %copy-done.21), kind=kOutput, calls=%fused_computation.37 | convolution fusion | flops 1074528256 | bytes 6291456 | tf_op jit(solution)/shard_map/dot_general | solution.py:11
  89.4 3.1 %convolution_convert_fusion.5 = bf16[32,16384]{1,0:T(8,128)(2,1)} fusion(bf16[64,16384]{1,0:T(8,128)(2,1)} %bitcast.3, s32[32]{0:T(128)S(1)} %add_bitcast_fusion), kind=kOutput, calls=%fused_computation.5 | convolution fusion | flops 67635200 | bytes 3145856 | tf_op jit(solution)/shard_map/dot_general | solution.py:106
  94.0 2.7 multiply_reduce_fusion
  96.7 1.8 multiply_reduce_fusion.1
  102.1 18.4 %all-to-all-done.1 = bf16[8,8,32,512]{3,1,2,0:T(8,128)(2,1)} async-done(((bf16[8,8,32,512]{3,1,2,0:T(8,128)(2,1)}), bf16[8,8,32,512]{3,1,2,0:T(8,128)(2,1)}, u32[]{:S(2)}, u32[]{:S(2)}) %all-to-all-start.1) | async-done | bytes 2097184 | tf_op jit(solution)/shard_map/all_to_all | solution.py:111
  120.5 3.1 %convolution_convert_fusion.4 = bf16[32,16384]{1,0:T(8,128)(2,1)} fusion(bf16[64,16384]{1,0:T(8,128)(2,1)} %bitcast.5, s32[32]{0:T(128)S(1)} %add_bitcast_fusion), kind=kOutput, calls=%fused_computation.4 | convolution fusion | flops 67635200 | bytes 3145856 | tf_op jit(solution)/shard_map/dot_general | solution.py:106
  123.6 2.3 reshape.130
  125.9 2.1 fusion.31
  132.0 3.3 %multiply_reduce_fusion.10 = (f32[512]{0:T(512)}, f32[512]{0:T(512)}, f32[512]{0:T(512)S(1)}, f32[512]{0:T(512)}, f32[512]{0:T(512)S(1)}, /*index=5*/f32[512]{0:...) fusion(f32[512,512]{0,1:T(8,128)S(1)} %copy-done.76, f32[]{:T(128)S(6)} %sub.91, ...), kind=kOutput, calls=%fused_computation.151 | convolution fusion | flops 69268480 | bytes 4342800 | tf_op jit(solution)/shard_map/dot_general | solution.py:36
  149.2 3.4 %fusion.71 = f32[512,2048]{1,0:T(8,128)} fusion(bf16[512,2048]{1,0:T(8,128)(2,1)S(1)} %copy-done, f32[512,128]{0,1:T(8,128)S(1)} %get-tuple-element.35, f32[512,128]{0,1:T(8,128)S(1)} %get-tuple-element.34, f32[512,128]{0,1:T(8,128)S(1)} %get-tuple-element.36, f32[512,128]{0,1:T(8,128)S(1)} %get-tuple-element.37, s32[512,512]{0,1:T(8,128)S(1)} %copy-done.22), kind=kOutput, calls=%fused_computation.132 | convolution fusion | flops 1075576832 | bytes 8388608 | tf_op jit(solution)/shard_map/dot_general | solution.py:144
  155.1 2.2 convolution_convert_fusion.1
  157.3 3.8 %all-to-all-start.2 = ((bf16[8,8,32,512]{3,1,2,0:T(8,128)(2,1)}), bf16[8,8,32,512]{3,1,2,0:T(8,128)(2,1)S(1)}, u32[]{:S(2)}, u32[]{:S(2)}) async-start(bf16[8,8,32,512]{3,1,2,0:T(8,128)(2,1)} %bitcast.83), calls=%async_computation.3 | async-start | bytes 4194304 | tf_op jit(solution)/shard_map/all_to_all | solution.py:200
  161.2 1.8 convolution_convert_fusion.19
  165.8 2.0 copy.55
  167.9 3.3 %convolution_convert_fusion.8 = bf16[1024,128]{0,1:T(8,128)(2,1)S(1)} fusion(f32[1024,512]{1,0:T(8,128)} %get-tuple-element.47, f32[512]{0:T(512)S(1)} %copy-done.68, f32[512]{0:T(512)S(1)} %copy-done.48, f32[512,512]{0,1:T(8,128)} %copy-done.75, f32[]{:T(128)} %bitcast.8), kind=kOutput, calls=%fused_computation.70 | convolution fusion | flops 136577024 | bytes 2626048 | tf_op jit(solution)/shard_map/dot_general | solution.py:17
  176.7 2.3 copy.52
  179.0 2.3 reshape.135
  184.6 2.3 fusion.33
  186.8 2.1 convolution_convert_fusion
  189.0 20.5 %all-to-all-done.2 = bf16[8,8,32,512]{3,1,2,0:T(8,128)(2,1)S(1)} async-done(((bf16[8,8,32,512]{3,1,2,0:T(8,128)(2,1)}), bf16[8,8,32,512]{3,1,2,0:T(8,128)(2,1)S(1)}, u32[]{:S(2)}, u32[]{:S(2)}) %all-to-all-start.2) | async-done | bytes 2097184 | tf_op jit(solution)/shard_map/all_to_all | solution.py:200
  209.5 4.5 %all-to-all-start.3 = ((bf16[8,8,32,512]{3,1,2,0:T(8,128)(2,1)}), bf16[8,8,32,512]{3,1,2,0:T(8,128)(2,1)}, u32[]{:S(2)}, u32[]{:S(2)}) async-start(bf16[8,8,32,512]{3,1,2,0:T(8,128)(2,1)} %bitcast.82), calls=%async_computation.4 | async-start | bytes 4194304 | tf_op jit(solution)/shard_map/all_to_all | solution.py:207
  215.4 1.8 fusion.34
  220.7 2.0 copy.54
  230.7 31.1 %all-to-all-done.3 = bf16[8,8,32,512]{3,1,2,0:T(8,128)(2,1)} async-done(((bf16[8,8,32,512]{3,1,2,0:T(8,128)(2,1)}), bf16[8,8,32,512]{3,1,2,0:T(8,128)(2,1)}, u32[]{:S(2)}, u32[]{:S(2)}) %all-to-all-start.3) | async-done | bytes 2097184 | tf_op jit(solution)/shard_map/all_to_all | solution.py:207
  261.8 2.2 convolution_convert_fusion.6
  265.0 2.1 convert_element_type.216
  (250 shorter events, 69.6 us)
Async XLA Ops:
  7.2 78.2 %copy-start = (bf16[512,2048]{1,0:T(8,128)(2,1)S(1)}, bf16[512,2048]{1,0:T(8,128)(2,1)}, u32[]{:S(2)}) copy-start(bf16[512,2048]{1,0:T(8,128)(2,1)} %param.18) | copy-start | bytes 6291460
  12.6 9.5 %copy-start.74 = (f32[4]{0:T(128)S(1)}, f32[4]{0:T(128)}, u32[]{:S(2)}) copy-start(f32[4]{0:T(128)} %param.16) | copy-start | bytes 52
  12.6 10.2 %copy-start.9 = (bf16[512,512]{1,0:T(8,128)(2,1)S(1)}, bf16[512,512]{1,0:T(8,128)(2,1)}, u32[]{:S(2)}) copy-start(bf16[512,512]{1,0:T(8,128)(2,1)} %param.10) | copy-start | bytes 1572868
  12.6 55.8 %all-to-all-start = ((bf16[8,8,32,512]{3,1,2,0:T(8,128)(2,1)}), bf16[8,8,32,512]{3,1,2,0:T(8,128)(2,1)}, u32[]{:S(2)}, u32[]{:S(2)}) async-start(bf16[8,8,32,512]{3,1,2,0:T(8,128)(2,1)} %bitcast.85), calls=%async_computation | async-start | bytes 4194304 | tf_op jit(solution)/shard_map/all_to_all | solution.py:110
  20.0 65.4 %all-gather.2.cloned.1.call-start = ((), (), s32[]{:S(2)}) async-start(), calls=%async_computation.6 | async-start | bytes 2621440 | tf_op jit(solution)/shard_map/all_gather | solution.py:148
  24.0 64.3 %copy-start.49 = (f32[512]{0:T(512)}, f32[512]{0:T(512)S(1)}, u32[]{:S(2)}) copy-start(f32[512]{0:T(512)S(1)} %get-tuple-element.52) | copy-start | bytes 6148
  25.2 63.2 %copy-start.51 = (f32[512]{0:T(512)}, f32[512]{0:T(512)S(1)}, u32[]{:S(2)}) copy-start(f32[512]{0:T(512)S(1)} %fusion.59) | copy-start | bytes 6148
  26.5 104.4 %copy-start.55 = (f32[512]{0:T(512)}, f32[512]{0:T(512)S(1)}, u32[]{:S(2)}) copy-start(f32[512]{0:T(512)S(1)} %get-tuple-element.42) | copy-start | bytes 6148
  27.8 55.5 %copy-start.53 = (f32[512]{0:T(512)}, f32[512]{0:T(512)S(1)}, u32[]{:S(2)}) copy-start(f32[512]{0:T(512)S(1)} %get-tuple-element.44) | copy-start | bytes 6148
  68.4 52.2 %all-to-all-start.1 = ((bf16[8,8,32,512]{3,1,2,0:T(8,128)(2,1)}), bf16[8,8,32,512]{3,1,2,0:T(8,128)(2,1)}, u32[]{:S(2)}, u32[]{:S(2)}) async-start(bf16[8,8,32,512]{3,1,2,0:T(8,128)(2,1)} %bitcast.84), calls=%async_computation.1 | async-start | bytes 4194304 | tf_op jit(solution)/shard_map/all_to_all | solution.py:111
  72.7 192.3 %reduce-scatter.2.cloned.1.call-start = ((), (), s32[]{:S(2)}) async-start(), calls=%async_computation.5 | async-start | bytes 5242880 | tf_op jit(solution)/shard_map/reduce_scatter | solution.py:145
  77.7 4.5 %copy-start.30 = (f32[512,512]{0,1:T(8,128)S(1)}, f32[512,512]{0,1:T(8,128)}, u32[]{:S(2)}) copy-start(f32[512,512]{0,1:T(8,128)} %copy-done.29) | copy-start | bytes 3145732
  77.7 4.5 %copy-start.73 = (bf16[512,512]{1,0:T(8,128)(2,1)S(1)}, bf16[512,512]{1,0:T(8,128)(2,1)}, u32[]{:S(2)}) copy-start(bf16[512,512]{1,0:T(8,128)(2,1)} %param.12) | copy-start | bytes 1572868
  79.3 51.6 %copy-start.63 = (f32[512]{0:T(512)}, f32[512]{0:T(512)S(1)}, u32[]{:S(2)}) copy-start(f32[512]{0:T(512)S(1)} %fusion.56) | copy-start | bytes 6148
  96.7 39.9 %copy-start.47 = (f32[512]{0:T(512)}, f32[512]{0:T(512)S(1)}, u32[]{:S(2)}) copy-start(f32[512]{0:T(512)S(1)} %get-tuple-element.46) | copy-start | bytes 6148
  98.6 36.8 %copy-start.45 = (f32[512]{0:T(512)}, f32[512]{0:T(512)S(1)}, u32[]{:S(2)}) copy-start(f32[512]{0:T(512)S(1)} %get-tuple-element.50) | copy-start | bytes 6148
  128.2 8.5 %copy-start.67 = (f32[512]{0:T(512)}, f32[512]{0:T(512)S(1)}, u32[]{:S(2)}) copy-start(f32[512]{0:T(512)S(1)} %fusion.31) | copy-start | bytes 6148
  130.2 5.1 %copy-start.65 = (f32[512]{0:T(512)}, f32[512]{0:T(512)S(1)}, u32[]{:S(2)}) copy-start(f32[512]{0:T(512)S(1)} %fusion.28) | copy-start | bytes 6148
  140.4 3.8 %copy-start.71 = (f32[512]{0:T(512)}, f32[512]{0:T(512)S(1)}, u32[]{:S(2)}) copy-start(f32[512]{0:T(512)S(1)} %fusion.25) | copy-start | bytes 6148
  157.3 3.8 %copy-start.56 = (f32[512]{0:T(512)S(1)}, f32[512]{0:T(512)}, u32[]{:S(2)}) copy-start(f32[512]{0:T(512)} %copy-done.55) | copy-start | bytes 6148
  157.3 3.9 %copy-start.64 = (f32[512]{0:T(512)S(1)}, f32[512]{0:T(512)}, u32[]{:S(2)}) copy-start(f32[512]{0:T(512)} %copy-done.63) | copy-start | bytes 6148
  157.3 52.2 %all-to-all-start.2 = ((bf16[8,8,32,512]{3,1,2,0:T(8,128)(2,1)}), bf16[8,8,32,512]{3,1,2,0:T(8,128)(2,1)S(1)}, u32[]{:S(2)}, u32[]{:S(2)}) async-start(bf16[8,8,32,512]{3,1,2,0:T(8,128)(2,1)} %bitcast.83), calls=%async_computation.3 | async-start | bytes 4194304 | tf_op jit(solution)/shard_map/all_to_all | solution.py:200
  167.8 3.3 %copy-start.7 = (f32[1024,512]{1,0:T(8,128)S(1)}, f32[1024,512]{1,0:T(8,128)}, u32[]{:S(2)}) copy-start(f32[1024,512]{1,0:T(8,128)} %get-tuple-element.51) | copy-start | bytes 6291460
  167.8 3.3 %copy-start.46 = (f32[512]{0:T(512)S(1)}, f32[512]{0:T(512)}, u32[]{:S(2)}) copy-start(f32[512]{0:T(512)} %copy-done.45) | copy-start | bytes 6148
  167.8 3.3 %copy-start.66 = (f32[512]{0:T(512)S(1)}, f32[512]{0:T(512)}, u32[]{:S(2)}) copy-start(f32[512]{0:T(512)} %copy-done.65) | copy-start | bytes 6148
  167.9 3.3 %copy-start.78 = (f32[512,512]{0,1:T(8,128)S(1)}, f32[512,512]{0,1:T(8,128)}, u32[]{:S(2)}) copy-start(f32[512,512]{0,1:T(8,128)} %copy-done.75) | copy-start | bytes 3145732
  176.7 4.6 %copy-start.85 = (f32[512]{0:T(512)S(1)}, f32[512]{0:T(512)}, u32[]{:S(2)}) copy-start(f32[512]{0:T(512)} %get-tuple-element.24) | copy-start | bytes 6148
  209.5 5.9 %copy-start.83 = (f32[512]{0:T(512)S(1)}, f32[512]{0:T(512)}, u32[]{:S(2)}) copy-start(f32[512]{0:T(512)} %get-tuple-element.27) | copy-start | bytes 6148
  209.5 52.3 %all-to-all-start.3 = ((bf16[8,8,32,512]{3,1,2,0:T(8,128)(2,1)}), bf16[8,8,32,512]{3,1,2,0:T(8,128)(2,1)}, u32[]{:S(2)}, u32[]{:S(2)}) async-start(bf16[8,8,32,512]{3,1,2,0:T(8,128)(2,1)} %bitcast.82), calls=%async_computation.4 | async-start | bytes 4194304 | tf_op jit(solution)/shard_map/all_to_all | solution.py:207
  222.7 3.5 %copy-start.26 = (bf16[512,512]{0,1:T(8,128)(2,1)S(1)}, bf16[512,512]{0,1:T(8,128)(2,1)}, u32[]{:S(2)}) copy-start(bf16[512,512]{0,1:T(8,128)(2,1)} %copy-done.25) | copy-start | bytes 1572868
  222.7 3.5 %copy-start.44 = (bf16[512,512]{1,0:T(8,128)(2,1)S(1)}, bf16[512,512]{1,0:T(8,128)(2,1)}, u32[]{:S(2)}) copy-start(bf16[512,512]{1,0:T(8,128)(2,1)} %param.11) | copy-start | bytes 1572868
  261.8 5.3 %copy-start.1 = (bf16[512,2048]{1,0:T(8,128)(2,1)S(1)}, bf16[512,2048]{1,0:T(8,128)(2,1)}, u32[]{:S(2)}) copy-start(bf16[512,2048]{1,0:T(8,128)(2,1)} %param.18) | copy-start | bytes 6291460
  (60 other events, 117.4 us)
Sparse Core Ops, SparseCore 0:
  22.4 23.9 all-gather.1
  152.8 43.4 reduce-scatter.1
where the time goes:
time: 276 us; the launch traced here: 274 us
  waiting for transfers between devices  109 us (39%)
  matrix products  82.7 us (30%)
  local copies, waits for them, and re-layouts  30.8 us (11%)
  starting transfers between devices  20.2 us (7%)
  between operations  17.6 us (6%)
  other arithmetic  13.5 us (5%)
    all_to_all x1, waiting for transfers between devices, per_device(): lax.all_to_all(outgoing(memory_keys), 'mem', split_axis=0, concat_axis=0,...  38.5 us
    all_to_all x1, waiting for transfers between devices, per_device(): lax.all_to_all(send_values.reshape(mem_count, capacity, block_len, featur...  31.1 us
    dot_general x17, matrix products, contract_last(): lax.dot_general(left, right, (((1,), (1,)), ((), ())), preferred_element_...  28.6 us
    dot_general x20, matrix products, contract_first(): lax.dot_general(left, right, (((0,), (0,)), ((), ())), preferred_element_...  24.6 us
    all_to_all x1, waiting for transfers between devices, per_device(): lax.all_to_all(send_keys.reshape(mem_count, capacity, block_len, feature_...  20.5 us
    unnamed x180, local copies, waits for them, and re-layouts  20.2 us
    all_to_all x1, waiting for transfers between devices, per_device(): lax.all_to_all(outgoing(memory_values), 'mem', split_axis=0, concat_axis=...  18.4 us
    dot_general x8, matrix products, branch_forward(): jnp.dot(weights.astype(jnp.bfloat16), valueset, preferred_element_type=jn...  10.8 us
  transfers between devices with their start and end apart: 6, of which 4 were waited for; matrix products, arithmetic and copies ran while one was open for 30% of the time, Pallas kernels for 0%

commit v1 on v0

--- a/solution.py
+++ b/solution.py
@@ -106,9 +106,28 @@
         chosen = jnp.dot(pick_table, flat_rows, preferred_element_type=jnp.float32)
         return chosen.astype(jnp.bfloat16).reshape(top_blocks * block_len, feature_cols)
 
+    def wrap_packet(state, ndim_at, where_dim=0):
+        upper, long_array = (lax.axis_size("mem"), lax.axis_index("mem"))
+        y = state.shape[ndim_at] // upper
+        n_now = list(state.shape)
+        n_now[ndim_at] = y
+        aux = n_now[where_dim]
+        n_now[where_dim] = aux * upper
+        local_next = jnp.zeros(n_now, state.dtype)
+        for nth in range(upper):
+            p_next = lax.dynamic_slice_in_dim(state, (long_array ^ nth) * y, y, axis=ndim_at)
+            if nth:
+                p_next = lax.ppermute(
+                    p_next, "mem", [(src_i, src_i ^ nth) for src_i in range(upper)]
+                )
+            local_next = lax.dynamic_update_slice_in_dim(
+                local_next, p_next, (long_array ^ nth) * aux, axis=where_dim
+            )
+        return local_next
+
     fetched = (
         lax.all_to_all(outgoing(memory_keys), "mem", split_axis=0, concat_axis=0, tiled=True),
-        lax.all_to_all(outgoing(memory_values), "mem", split_axis=0, concat_axis=0, tiled=True),
+        wrap_packet(outgoing(memory_values), 0),
     )
     gate_values = 1.0 / (1.0 + jnp.exp(-gate_logit))
     keep_mask = dropout_keep.astype(jnp.float32)

time: 276 us -> 282 us (1.022)
  starting transfers between devices: 20.2 us -> 33.2 us
  matrix products: 82.7 us -> 72.3 us
  local copies, waits for them, and re-layouts: 30.8 us -> 39.6 us
  other arithmetic: 13.5 us -> 9.66 us
    ppermute x0 -> x7, waiting for transfers between devices: none -> 56.5 us  [wrap_packet(): lax.ppermute(p_next, 'mem', [(src_i, src_i ^ nth) for src_i in range(uppe...]
    all_to_all x1, waiting for transfers between devices: 38.5 us -> 0.01 us  [per_device(): lax.all_to_all(outgoing(memory_keys), 'mem', split_axis=0, concat_axis=0,...]
    all_to_all x1 -> x0, waiting for transfers between devices: 18.4 us -> none  [per_device(): lax.all_to_all(outgoing(memory_values), 'mem', split_axis=0, concat_axis=...]
    ppermute x0 -> x7, starting transfers between devices: none -> 17.2 us  [wrap_packet(): lax.ppermute(p_next, 'mem', [(src_i, src_i ^ nth) for src_i in range(uppe...]
    dynamic_update_slice x0 -> x7, local copies, waits for them, and re-layouts: none -> 9.88 us  [wrap_packet(): lax.dynamic_update_slice_in_dim(local_next, p_next, (long_array ^ nth) *...]
    dot_general x17, matrix products: 28.6 us -> 19.8 us  [contract_last(): lax.dot_general(left, right, (((1,), (1,)), ((), ())), preferred_element_...]
    all_to_all x1 -> x0, starting transfers between devices: 4.34 us -> none  [per_device(): lax.all_to_all(outgoing(memory_values), 'mem', split_axis=0, concat_axis=...]
    reduce_sum x8, other arithmetic: 6.68 us -> 2.98 us  [branch_forward(): row_total = jnp.sum(weights, axis=1, keepdims=True)]
  transfers between devices with their start and end apart: 6 -> 12, of which waited for: 4 -> 6; matrix products, arithmetic and copies ran while one was open for 30% -> 29% of each run, Pallas kernels for 0% -> 0%
where the time goes in v1:
time: 282 us; the launch traced here: 281 us
  waiting for transfers between devices  108 us (38%)
  matrix products  72.3 us (26%)
  local copies, waits for them, and re-layouts  39.6 us (14%)
  starting transfers between devices  33.2 us (12%)
  between operations  17.9 us (6%)
  other arithmetic  9.66 us (3%)
    ppermute x7, waiting for transfers between devices, wrap_packet(): lax.ppermute(p_next, 'mem', [(src_i, src_i ^ nth) for src_i in range(uppe...  56.5 us
    all_to_all x1, waiting for transfers between devices, per_device(): lax.all_to_all(send_values.reshape(mem_count, capacity, block_len, featur...  31 us
    dot_general x20, matrix products, contract_first(): lax.dot_general(left, right, (((0,), (0,)), ((), ())), preferred_element_...  25 us
    dot_general x17, matrix products, contract_last(): lax.dot_general(left, right, (((1,), (1,)), ((), ())), preferred_element_...  19.8 us
    all_to_all x1, waiting for transfers between devices, per_device(): lax.all_to_all(send_keys.reshape(mem_count, capacity, block_len, feature_...  19.7 us
    unnamed x194, local copies, waits for them, and re-layouts  18.9 us
    ppermute x7, starting transfers between devices, wrap_packet(): lax.ppermute(p_next, 'mem', [(src_i, src_i ^ nth) for src_i in range(uppe...  17.2 us
    dynamic_update_slice x7, local copies, waits for them, and re-layouts, wrap_packet(): lax.dynamic_update_slice_in_dim(local_next, p_next, (long_array ^ nth) *...  9.88 us
  transfers between devices with their start and end apart: 12, of which 6 were waited for; matrix products, arithmetic and copies ran while one was open for 29% of the time, Pallas kernels for 0%

profile of v1, /device:TPU:0, one launch (start us, length us, event | category | flops | bytes accessed | tf_op | source)
XLA Modules:
  0.0 280.6 jit_solution(1370060497834902825)
XLA Ops:
  11.1 2.1 convolution_convert_fusion.3
  13.2 7.4 %all-to-all-start = ((bf16[8,8,32,512]{3,1,2,0:T(8,128)(2,1)}), bf16[8,8,32,512]{3,1,2,0:T(8,128)(2,1)}, u32[]{:S(2)}, u32[]{:S(2)}) async-start(bf16[8,8,32,512]{3,1,2,0:T(8,128)(2,1)} %bitcast.82), calls=%async_computation | async-start | bytes 4194304 | tf_op jit(solution)/shard_map/all_to_all | solution.py:129
  21.0 2.1 convolution_convert_fusion.2
  25.9 4.6 %collective-permute-start.6 = (bf16[1,8,32,512]{3,1,2,0:T(8,128)(2,1)S(1)}, bf16[1,8,32,512]{3,1,2,0:T(8,128)(2,1)}, u32[]{:S(2)}, u32[]{:S(2)}) collective-permute-start(bf16[1,8,32,512]{3,1,2,0:T(8,128)(2,1)S(1)} %get-tuple-element.34), channel_id=1, source_target_pairs={{0,28},{4,24},{8,20},{12,16},{16,12},{20,8},{24,4},{28,0},{1,29},{... | collective-permute-start | bytes 786440 | tf_op jit(solution)/shard_map/ppermute | solution.py:120
  32.7 1.9 collective-permute-start
  49.1 30.2 %collective-permute-done.1 = bf16[1,8,32,512]{3,1,2,0:T(8,128)(2,1)} collective-permute-done((bf16[1,8,32,512]{3,1,2,0:T(8,128)(2,1)}, bf16[1,8,32,512]{3,1,2,0:T(8,128)(2,1)}, u32[]{:S(2)}, u32[]{:S(2)}) %collective-permute-start.1) | collective-permute-done | bytes 262176 | tf_op jit(solution)/shard_map/ppermute | solution.py:120
  79.3 6.8 %collective-permute-start.4 = (bf16[1,8,32,512]{3,1,2,0:T(8,128)(2,1)}, bf16[1,8,32,512]{3,1,2,0:T(8,128)(2,1)S(1)}, u32[]{:S(2)}, u32[]{:S(2)}) collective-permute-start(bf16[1,8,32,512]{3,1,2,0:T(8,128)(2,1)} %get-tuple-element.36), channel_id=1, source_target_pairs={{0,20},{4,16},{8,28},{12,24},{16,4},{20,0},{24,12},{28,8},{1,21},{... | collective-permute-start | bytes 786440 | tf_op jit(solution)/shard_map/ppermute | solution.py:120
  89.4 20.1 %collective-permute-done.3 = bf16[1,8,32,512]{3,1,2,0:T(8,128)(2,1)S(1)} collective-permute-done((bf16[1,8,32,512]{3,1,2,0:T(8,128)(2,1)}, bf16[1,8,32,512]{3,1,2,0:T(8,128)(2,1)S(1)}, u32[]{:S(2)}, u32[]{:S(2)}) %collective-permute-start.3) | collective-permute-done | bytes 262176 | tf_op jit(solution)/shard_map/ppermute | solution.py:120
  110.3 6.1 %collective-permute-done.4 = bf16[1,8,32,512]{3,1,2,0:T(8,128)(2,1)S(1)} collective-permute-done((bf16[1,8,32,512]{3,1,2,0:T(8,128)(2,1)}, bf16[1,8,32,512]{3,1,2,0:T(8,128)(2,1)S(1)}, u32[]{:S(2)}, u32[]{:S(2)}) %collective-permute-start.4) | collective-permute-done | bytes 262176 | tf_op jit(solution)/shard_map/ppermute | solution.py:120
  120.5 2.1 convolution_convert_fusion.4
  123.9 3.2 %fusion.8 = f32[512,512]{0,1:T(8,128)S(1)} fusion(bf16[512,2048]{1,0:T(8,128)(2,1)} %all-gather.2.cloned.1.call-done, bf16[512,2048]{1,0:T(8,128)(2,1)S(1)} %copy-done, s32[512,512]{0,1:T(8,128)} %copy.42), kind=kOutput, calls=%fused_computation.37 | convolution fusion | flops 1074528256 | bytes 6291456 | tf_op jit(solution)/shard_map/dot_general | solution.py:11
  128.5 3.1 %convolution_convert_fusion.5 = bf16[32,16384]{1,0:T(8,128)(2,1)} fusion(bf16[64,16384]{1,0:T(8,128)(2,1)} %bitcast.3, s32[32]{0:T(128)S(1)} %fusion.184), kind=kOutput, calls=%fused_computation.5 | convolution fusion | flops 67635200 | bytes 3145856 | tf_op jit(solution)/shard_map/dot_general | solution.py:106
  140.4 3.3 %multiply_reduce_fusion.10 = (f32[512]{0:T(512)}, f32[512]{0:T(512)}, f32[512]{0:T(512)S(1)}, f32[512]{0:T(512)}, f32[512]{0:T(512)S(1)}, /*index=5*/f32[512]{0:...) fusion(f32[512,512]{0,1:T(8,128)S(1)} %copy-done.83, f32[]{:T(128)S(6)} %sub.91, ...), kind=kOutput, calls=%fused_computation.152 | convolution fusion | flops 69268480 | bytes 4342800 | tf_op jit(solution)/shard_map/dot_general | solution.py:36
  149.5 1.8 multiply_reduce_fusion.11
  156.4 3.3 %fusion.71 = f32[512,2048]{1,0:T(8,128)} fusion(bf16[512,2048]{1,0:T(8,128)(2,1)S(1)} %copy-done, f32[512,128]{0,1:T(8,128)S(1)} %get-tuple-element.43, f32[512,128]{0,1:T(8,128)S(1)} %get-tuple-element.42, f32[512,128]{0,1:T(8,128)S(1)} %get-tuple-element.44, f32[512,128]{0,1:T(8,128)S(1)} %get-tuple-element.45, s32[512,512]{0,1:T(8,128)S(1)} %copy-done.22), kind=kOutput, calls=%fused_computation.132 | convolution fusion | flops 1075576832 | bytes 8388608 | tf_op jit(solution)/shard_map/dot_general | solution.py:163
  162.0 2.2 convolution_convert_fusion.1
  164.3 4.0 %all-to-all-start.1 = ((bf16[8,8,32,512]{3,1,2,0:T(8,128)(2,1)}), bf16[8,8,32,512]{3,1,2,0:T(8,128)(2,1)S(1)}, u32[]{:S(2)}, u32[]{:S(2)}) async-start(bf16[8,8,32,512]{3,1,2,0:T(8,128)(2,1)} %bitcast.85), calls=%async_computation.2 | async-start | bytes 4194304 | tf_op jit(solution)/shard_map/all_to_all | solution.py:219
  168.3 1.8 convolution_convert_fusion.19
  172.8 2.0 copy.55
  174.9 3.5 %convolution_convert_fusion.8 = bf16[1024,128]{0,1:T(8,128)(2,1)S(1)} fusion(f32[1024,512]{1,0:T(8,128)} %copy-done.9, f32[512]{0:T(512)} %copy-done.75, f32[512]{0:T(512)} %copy-done.49, f32[512,512]{0,1:T(8,128)} %copy-done.82, f32[]{:T(128)} %bitcast.8), kind=kOutput, calls=%fused_computation.70 | convolution fusion | flops 136577024 | bytes 2626048 | tf_op jit(solution)/shard_map/dot_general | solution.py:17
  184.0 2.3 copy.52
  186.3 2.3 reshape.135
  188.7 1.8 fusion.36
  192.0 2.2 fusion.33
  194.2 2.2 convolution_convert_fusion
  196.5 19.7 %all-to-all-done.1 = bf16[8,8,32,512]{3,1,2,0:T(8,128)(2,1)S(1)} async-done(((bf16[8,8,32,512]{3,1,2,0:T(8,128)(2,1)}), bf16[8,8,32,512]{3,1,2,0:T(8,128)(2,1)S(1)}, u32[]{:S(2)}, u32[]{:S(2)}) %all-to-all-start.1) | async-done | bytes 2097184 | tf_op jit(solution)/shard_map/all_to_all | solution.py:219
  216.2 4.5 %all-to-all-start.2 = ((bf16[8,8,32,512]{3,1,2,0:T(8,128)(2,1)}), bf16[8,8,32,512]{3,1,2,0:T(8,128)(2,1)}, u32[]{:S(2)}, u32[]{:S(2)}) async-start(bf16[8,8,32,512]{3,1,2,0:T(8,128)(2,1)} %bitcast.84), calls=%async_computation.3 | async-start | bytes 4194304 | tf_op jit(solution)/shard_map/all_to_all | solution.py:226
  222.2 1.8 fusion.34
  227.4 2.0 copy.54
  237.4 31.0 %all-to-all-done.2 = bf16[8,8,32,512]{3,1,2,0:T(8,128)(2,1)} async-done(((bf16[8,8,32,512]{3,1,2,0:T(8,128)(2,1)}), bf16[8,8,32,512]{3,1,2,0:T(8,128)(2,1)}, u32[]{:S(2)}, u32[]{:S(2)}) %all-to-all-start.2) | async-done | bytes 2097184 | tf_op jit(solution)/shard_map/all_to_all | solution.py:226
  268.5 2.2 convolution_convert_fusion.6
  271.7 2.1 convert_element_type.216
  (285 shorter events, 76.4 us)
Async XLA Ops:
  7.2 116.8 %copy-start = (bf16[512,2048]{1,0:T(8,128)(2,1)S(1)}, bf16[512,2048]{1,0:T(8,128)(2,1)}, u32[]{:S(2)}) copy-start(bf16[512,2048]{1,0:T(8,128)(2,1)} %param.18) | copy-start | bytes 6291460
  7.2 116.8 %all-gather.2.cloned.1.call-start = ((), (), s32[]{:S(2)}) async-start(), calls=%async_computation.5 | async-start | bytes 2621440 | tf_op jit(solution)/shard_map/all_gather | solution.py:167
  13.2 7.5 %copy-start.44 = (bf16[16,32,512]{2,1,0:T(8,128)(2,1)S(1)}, bf16[16,32,512]{2,1,0:T(8,128)(2,1)}, u32[]{:S(2)}) copy-start(bf16[16,32,512]{2,1,0:T(8,128)(2,1)} %param.14) | copy-start | bytes 1572868
  13.2 115.4 %all-to-all-start = ((bf16[8,8,32,512]{3,1,2,0:T(8,128)(2,1)}), bf16[8,8,32,512]{3,1,2,0:T(8,128)(2,1)}, u32[]{:S(2)}, u32[]{:S(2)}) async-start(bf16[8,8,32,512]{3,1,2,0:T(8,128)(2,1)} %bitcast.82), calls=%async_computation | async-start | bytes 4194304 | tf_op jit(solution)/shard_map/all_to_all | solution.py:129
  20.6 251.1 %reduce-scatter.2.cloned.1.call-start = ((), (), s32[]{:S(2)}) async-start(), calls=%async_computation.4 | async-start | bytes 5242880 | tf_op jit(solution)/shard_map/reduce_scatter | solution.py:164
  24.7 9.9 %copy-start.11 = (bf16[512,512]{1,0:T(8,128)(2,1)S(1)}, bf16[512,512]{1,0:T(8,128)(2,1)}, u32[]{:S(2)}) copy-start(bf16[512,512]{1,0:T(8,128)(2,1)} %param.10) | copy-start | bytes 1572868
  24.7 9.9 %copy-start.45 = (bf16[512,512]{1,0:T(8,128)(2,1)S(1)}, bf16[512,512]{1,0:T(8,128)(2,1)}, u32[]{:S(2)}) copy-start(bf16[512,512]{1,0:T(8,128)(2,1)} %param.11) | copy-start | bytes 1572868
  25.9 9.7 %copy-start.10 = (bf16[8,8,32,512]{3,1,2,0:T(8,128)(2,1)}, bf16[8,8,32,512]{3,1,2,0:T(8,128)(2,1)S(1)}, u32[]{:S(2)}) copy-start(bf16[8,8,32,512]{3,1,2,0:T(8,128)(2,1)S(1)} %get-tuple-element.41) | copy-start | bytes 6291460
  25.9 92.9 %collective-permute-start.6 = (bf16[1,8,32,512]{3,1,2,0:T(8,128)(2,1)S(1)}, bf16[1,8,32,512]{3,1,2,0:T(8,128)(2,1)}, u32[]{:S(2)}, u32[]{:S(2)}) collective-permute-start(bf16[1,8,32,512]{3,1,2,0:T(8,128)(2,1)S(1)} %get-tuple-element.34), channel_id=1, source_target_pairs={{0,28},{4,24},{8,20},{12,16},{16,12},{20,8},{24,4},{28,0},{1,29},{... | collective-permute-start | bytes 786440 | tf_op jit(solution)/shard_map/ppermute | solution.py:120
  30.5 86.6 %collective-permute-start.5 = (bf16[1,8,32,512]{3,1,2,0:T(8,128)(2,1)}, bf16[1,8,32,512]{3,1,2,0:T(8,128)(2,1)}, u32[]{:S(2)}, u32[]{:S(2)}) collective-permute-start(bf16[1,8,32,512]{3,1,2,0:T(8,128)(2,1)} %get-tuple-element.35), channel_id=1, source_target_pairs={{0,24},{4,28},{8,16},{12,20},{16,8},{20,12},{24,0},{28,4},{1,25},{... | collective-permute-start | bytes 786440 | tf_op jit(solution)/shard_map/ppermute | solution.py:120
  31.1 56.6 %collective-permute-start.2 = (bf16[1,8,32,512]{3,1,2,0:T(8,128)(2,1)}, bf16[1,8,32,512]{3,1,2,0:T(8,128)(2,1)}, u32[]{:S(2)}, u32[]{:S(2)}) collective-permute-start(bf16[1,8,32,512]{3,1,2,0:T(8,128)(2,1)} %get-tuple-element.38), channel_id=1, source_target_pairs={{0,12},{4,8},{8,4},{12,0},{16,28},{20,24},{24,20},{28,16},{1,13},{... | collective-permute-start | bytes 786440 | tf_op jit(solution)/shard_map/ppermute | solution.py:120
  31.1 48.2 %collective-permute-start.1 = (bf16[1,8,32,512]{3,1,2,0:T(8,128)(2,1)}, bf16[1,8,32,512]{3,1,2,0:T(8,128)(2,1)}, u32[]{:S(2)}, u32[]{:S(2)}) collective-permute-start(bf16[1,8,32,512]{3,1,2,0:T(8,128)(2,1)} %get-tuple-element.39), channel_id=1, source_target_pairs={{0,8},{4,12},{8,0},{12,4},{16,24},{20,28},{24,16},{28,20},{1,9},{5... | collective-permute-start | bytes 786440 | tf_op jit(solution)/shard_map/ppermute | solution.py:120
  32.7 13.1 %collective-permute-start = (bf16[1,8,32,512]{3,1,2,0:T(8,128)(2,1)}, bf16[1,8,32,512]{3,1,2,0:T(8,128)(2,1)}, u32[]{:S(2)}, u32[]{:S(2)}) collective-permute-start(bf16[1,8,32,512]{3,1,2,0:T(8,128)(2,1)} %get-tuple-element.40), channel_id=1, source_target_pairs={{0,4},{4,0},{8,12},{12,8},{16,20},{20,16},{24,28},{28,24},{1,5},{5... | collective-permute-start | bytes 786440 | tf_op jit(solution)/shard_map/ppermute | solution.py:120
  34.9 92.2 %copy-start.50 = (f32[512]{0:T(512)}, f32[512]{0:T(512)S(1)}, u32[]{:S(2)}) copy-start(f32[512]{0:T(512)S(1)} %get-tuple-element.60) | copy-start | bytes 6148
  35.9 91.3 %copy-start.52 = (f32[512]{0:T(512)}, f32[512]{0:T(512)S(1)}, u32[]{:S(2)}) copy-start(f32[512]{0:T(512)S(1)} %fusion.59) | copy-start | bytes 6148
  38.2 6.2 %copy-start.29 = (s32[512,512]{1,0:T(8,128)S(1)}, s32[512,512]{1,0:T(8,128)}, u32[]{:S(2)}) copy-start(s32[512,512]{1,0:T(8,128)} %param.17) | copy-start | bytes 3145732
  45.7 63.8 %collective-permute-start.3 = (bf16[1,8,32,512]{3,1,2,0:T(8,128)(2,1)}, bf16[1,8,32,512]{3,1,2,0:T(8,128)(2,1)S(1)}, u32[]{:S(2)}, u32[]{:S(2)}) collective-permute-start(bf16[1,8,32,512]{3,1,2,0:T(8,128)(2,1)} %get-tuple-element.37), channel_id=1, source_target_pairs={{0,16},{4,20},{8,24},{12,28},{16,0},{20,4},{24,8},{28,12},{1,17},{... | collective-permute-start | bytes 786440 | tf_op jit(solution)/shard_map/ppermute | solution.py:120
  79.3 37.1 %collective-permute-start.4 = (bf16[1,8,32,512]{3,1,2,0:T(8,128)(2,1)}, bf16[1,8,32,512]{3,1,2,0:T(8,128)(2,1)S(1)}, u32[]{:S(2)}, u32[]{:S(2)}) collective-permute-start(bf16[1,8,32,512]{3,1,2,0:T(8,128)(2,1)} %get-tuple-element.36), channel_id=1, source_target_pairs={{0,20},{4,16},{8,28},{12,24},{16,4},{20,0},{24,12},{28,8},{1,21},{... | collective-permute-start | bytes 786440 | tf_op jit(solution)/shard_map/ppermute | solution.py:120
  134.8 10.3 %copy-start.9 = (f32[1024,512]{1,0:T(8,128)}, f32[1024,512]{1,0:T(8,128)S(1)}, u32[]{:S(2)}) copy-start(f32[1024,512]{1,0:T(8,128)S(1)} %get-tuple-element.55) | copy-start | bytes 6291460
  134.8 10.3 %copy-start.49 = (f32[512]{0:T(512)}, f32[512]{0:T(512)S(1)}, u32[]{:S(2)}) copy-start(f32[512]{0:T(512)S(1)} %get-tuple-element.54) | copy-start | bytes 6148
  135.2 8.5 %copy-start.7 = (f32[1024,512]{1,0:T(8,128)}, f32[1024,512]{1,0:T(8,128)S(1)}, u32[]{:S(2)}) copy-start(f32[1024,512]{1,0:T(8,128)S(1)} %get-tuple-element.59) | copy-start | bytes 6291460
  135.2 8.5 %copy-start.47 = (f32[512]{0:T(512)}, f32[512]{0:T(512)S(1)}, u32[]{:S(2)}) copy-start(f32[512]{0:T(512)S(1)} %get-tuple-element.58) | copy-start | bytes 6148
  135.7 15.6 %copy-start.5 = (f32[1024,512]{1,0:T(8,128)}, f32[1024,512]{1,0:T(8,128)S(1)}, u32[]{:S(2)}) copy-start(f32[1024,512]{1,0:T(8,128)S(1)} %get-tuple-element.66) | copy-start | bytes 6291460
  136.2 16.5 %copy-start.3 = (f32[1024,512]{1,0:T(8,128)}, f32[1024,512]{1,0:T(8,128)S(1)}, u32[]{:S(2)}) copy-start(f32[1024,512]{1,0:T(8,128)S(1)} %get-tuple-element.64) | copy-start | bytes 6291460
  137.7 7.4 %copy-start.75 = (f32[512]{0:T(512)}, f32[512]{0:T(512)S(1)}, u32[]{:S(2)}) copy-start(f32[512]{0:T(512)S(1)} %fusion.31) | copy-start | bytes 6148
  138.6 5.1 %copy-start.73 = (f32[512]{0:T(512)}, f32[512]{0:T(512)S(1)}, u32[]{:S(2)}) copy-start(f32[512]{0:T(512)S(1)} %fusion.28) | copy-start | bytes 6148
  164.3 51.9 %all-to-all-start.1 = ((bf16[8,8,32,512]{3,1,2,0:T(8,128)(2,1)}), bf16[8,8,32,512]{3,1,2,0:T(8,128)(2,1)S(1)}, u32[]{:S(2)}, u32[]{:S(2)}) async-start(bf16[8,8,32,512]{3,1,2,0:T(8,128)(2,1)} %bitcast.85), calls=%async_computation.2 | async-start | bytes 4194304 | tf_op jit(solution)/shard_map/all_to_all | solution.py:219
  216.2 5.9 %copy-start.56 = (f32[512]{0:T(512)S(1)}, f32[512]{0:T(512)}, u32[]{:S(2)}) copy-start(f32[512]{0:T(512)} %copy-done.54) | copy-start | bytes 6148
  216.2 5.9 %copy-start.59 = (f32[512]{0:T(512)S(1)}, f32[512]{0:T(512)}, u32[]{:S(2)}) copy-start(f32[512]{0:T(512)} %copy-done.57) | copy-start | bytes 6148
  216.2 5.9 %copy-start.90 = (f32[512]{0:T(512)S(1)}, f32[512]{0:T(512)}, u32[]{:S(2)}) copy-start(f32[512]{0:T(512)} %get-tuple-element.27) | copy-start | bytes 6148
  216.2 52.3 %all-to-all-start.2 = ((bf16[8,8,32,512]{3,1,2,0:T(8,128)(2,1)}), bf16[8,8,32,512]{3,1,2,0:T(8,128)(2,1)}, u32[]{:S(2)}, u32[]{:S(2)}) async-start(bf16[8,8,32,512]{3,1,2,0:T(8,128)(2,1)} %bitcast.84), calls=%async_computation.3 | async-start | bytes 4194304 | tf_op jit(solution)/shard_map/all_to_all | solution.py:226
  268.5 5.3 %copy-start.1 = (bf16[512,2048]{1,0:T(8,128)(2,1)S(1)}, bf16[512,2048]{1,0:T(8,128)(2,1)}, u32[]{:S(2)}) copy-start(bf16[512,2048]{1,0:T(8,128)(2,1)} %param.18) | copy-start | bytes 6291460
  (73 other events, 169.0 us)
Sparse Core Ops, SparseCore 0:
  9.6 25.2 all-gather.1
  159.9 43.1 reduce-scatter.1
